TPU v7x, 128 devices: a whole 4x4x4 slice. The times are simulated.
128 devices in a mesh: ang: 4 (over y), pix: 32 (over x, z, core).
Axes of the slice: x: 4, y: 4, z: 4, core: 2. Of those that a mesh axis runs over, the one named last changes fastest.
Arguments:
- flats: float32 [256, 256, 4096], P(None, 'pix', 'ang'), may hold values from -60 to 60
- projections: float32 [128, 256, 4096], P('ang', None, 'pix'), may hold values from -60 to 60
- start_basis: float32 [256, 48], replicated, may hold values from -0.375 to 0.375
Outputs:
- corrected: float32 [128, 256, 4096], P('ang', None, 'pix')
All inputs are finite; a program needn't handle non-finite values.
Results may differ from a plain program's by a relative error of at most 0.0001.
Values sent between devices are 32-bit elements; how exact they have to be, the bound alone decides.
No kernel may reach another device: no remote copies, remote signals or barrier semaphores. Data moves between devices by JAX's collectives and lax.ppermute only.
A program may use at most 128 MiB of HBM per device.

v0:
```python
import jax
import jax.numpy as jnp
from jax import lax
from jax.sharding import PartitionSpec as P

SUBSPACE = 2
floor_value = 0.2


def orthonormal(grown):
    correlation = jnp.dot(grown.T, grown, precision=lax.Precision.HIGHEST)
    lower = jnp.linalg.cholesky(correlation)
    return jax.scipy.linalg.solve_triangular(lower, grown.T, lower=True).T


def solve_normal(normal, fit_rhs):
    factor = jnp.linalg.cholesky(normal)
    return jax.scipy.linalg.cho_solve((factor, True), fit_rhs.T).T


def shards(flats, projections, start_basis):
    frames_here, rows_dev, cols_dev = flats.shape
    npix = rows_dev * cols_dev * lax.axis_size("ang") * lax.axis_size("pix")
    mean_flat = jnp.mean(flats, axis=0)
    centered = (flats - mean_flat).reshape(frames_here, -1)
    local_gram = jnp.dot(centered, centered.T, precision=lax.Precision.HIGHEST)
    gram = lax.psum(local_gram, ("ang", "pix")) / npix
    basis = start_basis
    for turn in range(SUBSPACE):
        basis = orthonormal(jnp.dot(gram, basis, precision=lax.Precision.HIGHEST))
    eigen_flats = jnp.dot(basis.T, centered, precision=lax.Precision.HIGHEST)
    normal = jnp.dot(
        basis.T,
        jnp.dot(gram, basis, precision=lax.Precision.HIGHEST),
        precision=lax.Precision.HIGHEST,
    )
    eigen_count = eigen_flats.shape[0]
    tiles = lax.all_to_all(projections, "pix", split_axis=1, concat_axis=2, tiled=True)
    eigen_rows, mean_rows = (
        lax.all_gather(
            eigen_flats.reshape(eigen_count, rows_dev, cols_dev), "ang", axis=2, tiled=True
        ),
        lax.all_gather(mean_flat, "ang", axis=1, tiled=True),
    )
    angle_count = tiles.shape[0]
    frames = tiles.reshape(angle_count, -1)
    flat_row = mean_rows.reshape(1, -1)
    eigen_wide = eigen_rows.reshape(eigen_count, -1)
    partial_value = jnp.dot(frames - flat_row, eigen_wide.T, precision=lax.Precision.HIGHEST)
    fit_rhs = lax.psum(partial_value, "pix") / npix
    weights = solve_normal(normal, fit_rhs)
    estimate = flat_row + jnp.dot(weights, eigen_wide, precision=lax.Precision.HIGHEST)
    tiles_out = (frames / jnp.maximum(estimate, floor_value)).reshape(tiles.shape)
    result = lax.all_to_all(tiles_out, "pix", split_axis=2, concat_axis=1, tiled=True)
    return result


def solution(mesh):
    in_specs = (P(None, "pix", "ang"), P("ang", None, "pix"), P())
    out_specs = P("ang", None, "pix")
    return jax.shard_map(shards, mesh=mesh, in_specs=in_specs, out_specs=out_specs, check_vma=False)
```

profile of v0, /device:TPU:1, one launch (start us, length us, event | category | flops | bytes accessed | tf_op | source)
XLA Modules:
  0.0 571.3 jit_solution(11641598748296280)
XLA Ops:
  18.1 17.2 %fusion.7 = f32[256,256]{1,0:T(8,128)} fusion(f32[256,8,1024]{2,1,0:T(8,128)S(1)} %broadcast_subtract_fusion), kind=kOutput, calls=%fused_computation.10 | convolution fusion | flops 6442450944 | bytes 8650752 | tf_op jit(solution)/shard_map/dot_general | solution.py:26
  35.7 15.0 %copy.49 = f32[32,8,8,1024]{3,1,2,0:T(8,128)} copy(f32[32,8,8,1024]{3,2,1,0:T(8,128)} %bitcast.84) | data formatting | bytes 16777216
  50.8 9.2 %copy.41 = f32[8192,256]{1,0:T(8,128)} copy(f32[8192,256]{0,1:T(8,128)} %bitcast.88) | data formatting | bytes 16777216 | tf_op jit(solution)/shard_map/dot_general | solution.py:31
  59.9 120.3 %all-reduce.2.cloned.1.call-done = f32[256,256]{1,0:T(8,128)} async-done(((f32[256,256]{1,0:T(8,128)}), f32[256,256]{1,0:T(8,128)}) %all-reduce.2.cloned.1.call-update) | async-done | bytes 262160 | tf_op jit(solution)/shard_map/psum | solution.py:27
  181.8 4.4 cholesky.59
  193.1 4.4 cholesky.70
  202.7 12.2 %fusion.19 = f32[48,8,1024]{2,0,1:T(8,128)} fusion(f32[8,1024,256]{2,1,0:T(8,128)} %bitcast.87, f32[48,256]{1,0:T(8,128)S(1)} %fusion.21), kind=kOutput, calls=%fused_computation.20 | convolution fusion | flops 1207959552 | bytes 10010624 | tf_op jit(solution)/shard_map/dot_general | solution.py:31
  215.0 6.6 %copy.33 = f32[32,256,128]{2,0,1:T(8,128)} copy(f32[32,256,128]{2,1,0:T(8,128)} %param.7) | data formatting | bytes 8388608 | tf_op args[1]
  221.6 5.6 all-to-all-start
  227.2 11.0 %all_gather.6 = f32[8,4096]{1,0:T(8,128)S(1)} all-gather(f32[8,1024]{1,0:T(8,128)S(1)} %broadcast_multiply_fusion), channel_id=1, replica_groups=mesh['ang'=4,'pix'=32] {'ang'}, dimensions={1}, use_global_device_ids=true | all-gather | bytes 163840 | tf_op jit(solution)/shard_map/all_gather | solution.py:43
  238.9 4.4 cholesky.81
  248.4 31.1 %all-to-all-done = f32[32,256,128]{2,0,1:T(8,128)} async-done(((f32[32,256,128]{2,0,1:T(8,128)}), f32[32,256,128]{2,0,1:T(8,128)}, u32[]{:S(2)}, u32[]{:S(2)}) %all-to-all-start) | async-done | bytes 4194336 | tf_op jit(solution)/shard_map/all_to_all | solution.py:38
  279.5 6.7 %copy.34 = f32[32,32,8,128]{3,1,2,0:T(8,128)} copy(f32[32,32,8,128]{3,0,2,1:T(8,128)} %bitcast) | data formatting | bytes 8388608 | tf_op jit(solution)/shard_map/all_to_all | solution.py:38
  286.2 6.6 %bitcast_subtract_fusion = f32[32,8,32,128]{3,2,1,0:T(8,128)} fusion(f32[8,32,128]{2,1,0:T(8,128)S(1)} %copy.40, f32[32,32,8,128]{3,0,2,1:T(8,128)} %bitcast), kind=kLoop, calls=%fused_computation.8 | loop fusion | flops 1048576 | bytes 8519680 | tf_op jit(solution)/shard_map/sub | solution.py:49
  298.8 7.2 %fusion.4 = f32[32,48]{1,0:T(8,128)S(1)} fusion(f32[48,32768]{1,0:T(8,128)S(1)} %bitcast.89, f32[4,8,256,128]{3,2,1,0:T(8,128)S(1)} %bitcast.91), kind=kOutput, calls=%fused_computation.5 | convolution fusion | flops 603979776 | bytes 10491904 | tf_op jit(solution)/shard_map/dot_general | solution.py:49
  306.0 120.0 %psum.15 = f32[32,48]{1,0:T(8,128)S(1)} all-reduce(f32[32,48]{1,0:T(8,128)S(1)} %fusion.4), channel_id=1, replica_groups=mesh['ang'=4,'pix'=32] {'pix'}, use_global_device_ids=true, to_apply=%region_4.7 | all-reduce | flops 1536 | bytes 12288 | tf_op jit(solution)/shard_map/psum | solution.py:50
  426.4 9.0 %fusion.1 = f32[32,32768]{1,0:T(8,128)S(1)} fusion(f32[48,32]{0,1:T(8,128)S(1)} %fusion.28, f32[48,32768]{1,0:T(8,128)} %bitcast.90, f32[4,8,256,128]{3,2,1,0:T(8,128)} %bitcast.94, f32[32768]{0:T(1024)S(1)} %bitcast.98), kind=kOutput, calls=%fused_computation.2 | convolution fusion | flops 607125504 | bytes 14817280 | tf_op jit(solution)/shard_map/dot_general | solution.py:52
  435.4 4.4 copy.50
  439.9 10.8 %copy.43 = f32[32,8,4096]{0,1,2:T(8,128)} copy(f32[32,8,4096]{2,1,0:T(8,128)} %bitcast.92) | data formatting | bytes 8388608 | tf_op jit(solution)/shard_map/reshape | solution.py:53
  450.7 16.0 %reshape.47 = f32[32,1,32768]{2,1,0:T(1,128)} reshape(f32[4096,8,32]{2,1,0:T(8,128)} %bitcast.85) | data formatting | bytes 8388608
  466.7 61.1 %all_to_all.33 = f32[32,1,32768]{2,1,0:T(1,128)} all-to-all(f32[32,1,32768]{2,1,0:T(1,128)} %reshape.47), channel_id=1, replica_groups=mesh['ang'=4,'pix'=32] {'pix'}, dimensions={0} | all-to-all | bytes 8388608 | tf_op jit(solution)/shard_map/all_to_all | solution.py:54
  528.3 13.7 %reduce.4 = f32[32,32768]{1,0:T(8,128)} reduce(f32[32,1,32768]{2,1,0:T(1,128)} %all_to_all.33, f32[]{:T(128)} %broadcast.81), dimensions={1}, to_apply=%all_to_all.27.reduce_sub_computation | reduce | bytes 8388612 | tf_op jit(solution)/shard_map/all_to_all | solution.py:54
  542.1 9.8 %reshape.48 = f32[4096,8,32]{2,1,0:T(8,128)} reshape(f32[32,32768]{1,0:T(8,128)} %reduce.4) | data formatting | bytes 8388608
  551.9 12.1 %copy.44 = f32[32,32,8,128]{3,2,1,0:T(8,128)} copy(f32[32,32,8,128]{0,2,3,1:T(8,128)} %bitcast.86) | data formatting | bytes 8388608 | tf_op jit(solution)/shard_map/all_to_all | solution.py:54
  (52 shorter events, 38.2 us)
Async XLA Ops:
  6.5 173.7 %copy-start = (f32[256,48]{0,1:T(8,128)S(1)}, f32[256,48]{0,1:T(8,128)}, u32[]{:S(2)}) copy-start(f32[256,48]{0,1:T(8,128)} %param.8) | copy-start | bytes 147460
  6.5 173.7 %all-reduce.2.cloned.1.call-start = ((), (), s32[]{:S(2)}) async-start(), calls=%async_computation.2 | async-start | bytes 524288 | tf_op jit(solution)/shard_map/psum | solution.py:27
  14.8 3.2 copy-start.2
  35.3 257.5 %all-gather.2.cloned.1.call-start = ((), (), s32[]{:S(2)}) async-start(), calls=%async_computation.3 | async-start | bytes 7864320 | tf_op jit(solution)/shard_map/all_gather | solution.py:40
  221.6 16.6 %copy-start.5 = (f32[256,256]{1,0:T(8,128)S(1)}, f32[256,256]{1,0:T(8,128)}, u32[]{:S(2)}) copy-start(f32[256,256]{1,0:T(8,128)} %all-reduce.2.cloned.1.call-done) | copy-start | bytes 786436
  221.6 57.9 %all-to-all-start = ((f32[32,256,128]{2,0,1:T(8,128)}), f32[32,256,128]{2,0,1:T(8,128)}, u32[]{:S(2)}, u32[]{:S(2)}) async-start(f32[32,256,128]{2,0,1:T(8,128)} %copy.33), calls=%async_computation | async-start | bytes 8388608 | tf_op jit(solution)/shard_map/all_to_all | solution.py:38
  292.8 6.0 %copy-start.4 = (f32[32,8,32,128]{3,2,1,0:T(8,128)S(1)}, f32[32,8,32,128]{3,2,1,0:T(8,128)}, u32[]{:S(2)}) copy-start(f32[32,8,32,128]{3,2,1,0:T(8,128)} %bitcast_subtract_fusion) | copy-start | bytes 12582916
  296.2 2.7 copy-start.3
  551.9 12.1 %copy-start.1 = (f32[256,48]{0,1:T(8,128)S(1)}, f32[256,48]{0,1:T(8,128)}, u32[]{:S(2)}) copy-start(f32[256,48]{0,1:T(8,128)} %param.8) | copy-start | bytes 147460
Sparse Core Ops, SparseCore 0:
  35.4 144.7 all-reduce.1
  215.1 64.1 all-gather.1
where the time goes:
time: 581 us; the launch traced here: 571 us
  blocking collectives  192 us (33%)
  waiting for transfers between devices  151 us (26%)
  local copies, waits for them, and re-layouts  101 us (17%)
  other arithmetic  56.9 us (10%)
  matrix products  49.9 us (9%)
  between operations  14.1 us (2%)
  starting transfers between devices  6.04 us (1%)
    psum x1, waiting for transfers between devices, shards(): gram = lax.psum(local_gram, ('ang', 'pix')) / npix  120 us
    psum x1, blocking collectives, shards(): fit_rhs = lax.psum(partial_value, 'pix') / npix  120 us
    all_to_all x1, blocking collectives, shards(): lax.all_to_all(tiles_out, 'pix', split_axis=2, concat_axis=1, tiled=True)  61.1 us
    unnamed x18, local copies, waits for them, and re-layouts  57.8 us
    all_to_all x1, waiting for transfers between devices, shards(): lax.all_to_all(projections, 'pix', split_axis=1, concat_axis=2, tiled=True)  31.1 us
    dot_general x1, matrix products, shards(): local_gram = jnp.dot(centered, centered.T, precision=lax.Precision.HIGHEST)  17.2 us
    all_to_all x1, other arithmetic, shards(): lax.all_to_all(tiles_out, 'pix', split_axis=2, concat_axis=1, tiled=True)  13.7 us
    all_to_all x2, local copies, waits for them, and re-layouts, shards(): lax.all_to_all(tiles_out, 'pix', split_axis=2, concat_axis=1, tiled=True)  12.6 us
  transfers between devices with their start and end apart: 3, of which 2 were waited for; matrix products, arithmetic and copies ran while one was open for 10% of the time, Pallas kernels for 0%

commit v1 on v0

--- a/solution.py
+++ b/solution.py
@@ -5,6 +5,11 @@
 
 SUBSPACE = 2
 floor_value = 0.2
+
+
+def one_after_other(value, one, other):
+    inner = lax.psum(value, one)
+    return lax.psum(inner, other)
 
 
 def orthonormal(grown):
@@ -24,7 +29,7 @@
     mean_flat = jnp.mean(flats, axis=0)
     centered = (flats - mean_flat).reshape(frames_here, -1)
     local_gram = jnp.dot(centered, centered.T, precision=lax.Precision.HIGHEST)
-    gram = lax.psum(local_gram, ("ang", "pix")) / npix
+    gram = one_after_other(local_gram, "pix", "ang") / npix
     basis = start_basis
     for turn in range(SUBSPACE):
         basis = orthonormal(jnp.dot(gram, basis, precision=lax.Precision.HIGHEST))

time: 581 us -> 587 us (1.010)
    psum x1 -> x2, waiting for transfers between devices: 120 us -> 122 us  [the longest x1 105 us: one_after_other(): inner = lax.psum(value, one)]
  transfers between devices with their start and end apart: 3 -> 4, of which waited for: 2 -> 3; matrix products, arithmetic and copies ran while one was open for 10% -> 9% of each run, Pallas kernels for 0% -> 0%
where the time goes in v1:
time: 587 us; the launch traced here: 577 us
  blocking collectives  192 us (33%)
  waiting for transfers between devices  153 us (26%)
  local copies, waits for them, and re-layouts  101 us (17%)
  other arithmetic  56.9 us (10%)
  matrix products  49.9 us (9%)
  between operations  13.8 us (2%)
  starting transfers between devices  10.5 us (2%)
    psum x1, blocking collectives, shards(): fit_rhs = lax.psum(partial_value, 'pix') / npix  120 us
    psum x1, waiting for transfers between devices, one_after_other(): inner = lax.psum(value, one)  105 us
    all_to_all x1, blocking collectives, shards(): lax.all_to_all(tiles_out, 'pix', split_axis=2, concat_axis=1, tiled=True)  61.1 us
    unnamed x18, local copies, waits for them, and re-layouts  57.8 us
    all_to_all x1, waiting for transfers between devices, shards(): lax.all_to_all(projections, 'pix', split_axis=1, concat_axis=2, tiled=True)  31.1 us
    dot_general x1, matrix products, shards(): local_gram = jnp.dot(centered, centered.T, precision=lax.Precision.HIGHEST)  17.2 us
    psum x1, waiting for transfers between devices, one_after_other(): return lax.psum(inner, other)  16.8 us
    all_to_all x1, other arithmetic, shards(): lax.all_to_all(tiles_out, 'pix', split_axis=2, concat_axis=1, tiled=True)  13.7 us
  transfers between devices with their start and end apart: 4, of which 3 were waited for; matrix products, arithmetic and copies ran while one was open for 9% of the time, Pallas kernels for 0%

profile of v1, /device:TPU:1, one launch (start us, length us, event | category | flops | bytes accessed | tf_op | source)
XLA Modules:
  0.0 576.7 jit_solution(3775558492290017511)
XLA Ops:
  18.1 17.2 %fusion.7 = f32[256,256]{1,0:T(8,128)} fusion(f32[256,8,1024]{2,1,0:T(8,128)S(1)} %broadcast_subtract_fusion), kind=kOutput, calls=%fused_computation.10 | convolution fusion | flops 6442450944 | bytes 8650752 | tf_op jit(solution)/shard_map/dot_general | solution.py:31
  35.3 104.8 %all-reduce.3.cloned.1.call-done = f32[256,256]{1,0:T(8,128)} async-done(((f32[256,256]{1,0:T(8,128)}), f32[256,256]{1,0:T(8,128)}) %all-reduce.3.cloned.1.call-update) | async-done | bytes 262160 | tf_op jit(solution)/shard_map/psum | solution.py:11
  140.6 15.0 %copy.49 = f32[32,8,8,1024]{3,1,2,0:T(8,128)} copy(f32[32,8,8,1024]{3,2,1,0:T(8,128)} %bitcast.84) | data formatting | bytes 16777216
  155.6 9.2 %copy.41 = f32[8192,256]{1,0:T(8,128)} copy(f32[8192,256]{0,1:T(8,128)} %bitcast.88) | data formatting | bytes 16777216 | tf_op jit(solution)/shard_map/dot_general | solution.py:36
  164.8 16.8 %all-reduce.5.cloned.1.call-done = f32[256,256]{1,0:T(8,128)} async-done(((f32[256,256]{1,0:T(8,128)}), f32[256,256]{1,0:T(8,128)}) %all-reduce.5.cloned.1.call-update) | async-done | bytes 262160 | tf_op jit(solution)/shard_map/psum | solution.py:12
  183.2 4.4 cholesky.59
  194.5 4.4 cholesky.70
  204.1 12.2 %fusion.19 = f32[48,8,1024]{2,0,1:T(8,128)} fusion(f32[8,1024,256]{2,1,0:T(8,128)} %bitcast.87, f32[48,256]{1,0:T(8,128)S(1)} %fusion.21), kind=kOutput, calls=%fused_computation.20 | convolution fusion | flops 1207959552 | bytes 10010624 | tf_op jit(solution)/shard_map/dot_general | solution.py:36
  216.4 6.6 %copy.33 = f32[32,256,128]{2,0,1:T(8,128)} copy(f32[32,256,128]{2,1,0:T(8,128)} %param.7) | data formatting | bytes 8388608 | tf_op args[1]
  223.0 10.0 %all-to-all-start = ((f32[32,256,128]{2,0,1:T(8,128)}), f32[32,256,128]{2,0,1:T(8,128)}, u32[]{:S(2)}, u32[]{:S(2)}) async-start(f32[32,256,128]{2,0,1:T(8,128)} %copy.33), calls=%async_computation | async-start | bytes 8388608 | tf_op jit(solution)/shard_map/all_to_all | solution.py:43
  233.0 11.0 %all_gather.6 = f32[8,4096]{1,0:T(8,128)S(1)} all-gather(f32[8,1024]{1,0:T(8,128)S(1)} %broadcast_multiply_fusion), channel_id=1, replica_groups=mesh['ang'=4,'pix'=32] {'ang'}, dimensions={1}, use_global_device_ids=true | all-gather | bytes 163840 | tf_op jit(solution)/shard_map/all_gather | solution.py:48
  254.2 31.1 %all-to-all-done = f32[32,256,128]{2,0,1:T(8,128)} async-done(((f32[32,256,128]{2,0,1:T(8,128)}), f32[32,256,128]{2,0,1:T(8,128)}, u32[]{:S(2)}, u32[]{:S(2)}) %all-to-all-start) | async-done | bytes 4194336 | tf_op jit(solution)/shard_map/all_to_all | solution.py:43
  285.2 6.7 %copy.34 = f32[32,32,8,128]{3,1,2,0:T(8,128)} copy(f32[32,32,8,128]{3,0,2,1:T(8,128)} %bitcast) | data formatting | bytes 8388608 | tf_op jit(solution)/shard_map/all_to_all | solution.py:43
  291.9 6.6 %bitcast_subtract_fusion = f32[32,8,32,128]{3,2,1,0:T(8,128)} fusion(f32[8,32,128]{2,1,0:T(8,128)S(1)} %copy.40, f32[32,32,8,128]{3,0,2,1:T(8,128)} %bitcast), kind=kLoop, calls=%fused_computation.8 | loop fusion | flops 1048576 | bytes 8519680 | tf_op jit(solution)/shard_map/sub | solution.py:54
  304.6 7.2 %fusion.4 = f32[32,48]{1,0:T(8,128)S(1)} fusion(f32[48,32768]{1,0:T(8,128)S(1)} %bitcast.89, f32[4,8,256,128]{3,2,1,0:T(8,128)S(1)} %bitcast.91), kind=kOutput, calls=%fused_computation.5 | convolution fusion | flops 603979776 | bytes 10491904 | tf_op jit(solution)/shard_map/dot_general | solution.py:54
  311.7 120.0 %psum.23 = f32[32,48]{1,0:T(8,128)S(1)} all-reduce(f32[32,48]{1,0:T(8,128)S(1)} %fusion.4), channel_id=1, replica_groups=mesh['ang'=4,'pix'=32] {'pix'}, use_global_device_ids=true, to_apply=%region_5.8 | all-reduce | flops 1536 | bytes 12288 | tf_op jit(solution)/shard_map/psum | solution.py:55
  432.1 9.0 %fusion.1 = f32[32,32768]{1,0:T(8,128)S(1)} fusion(f32[48,32]{0,1:T(8,128)S(1)} %fusion.28, f32[48,32768]{1,0:T(8,128)} %bitcast.90, f32[4,8,256,128]{3,2,1,0:T(8,128)} %bitcast.94, f32[32768]{0:T(1024)S(1)} %bitcast.98), kind=kOutput, calls=%fused_computation.2 | convolution fusion | flops 607125504 | bytes 14817280 | tf_op jit(solution)/shard_map/dot_general | solution.py:57
  441.1 4.4 copy.50
  445.6 10.8 %copy.43 = f32[32,8,4096]{0,1,2:T(8,128)} copy(f32[32,8,4096]{2,1,0:T(8,128)} %bitcast.92) | data formatting | bytes 8388608 | tf_op jit(solution)/shard_map/reshape | solution.py:58
  456.4 16.0 %reshape.47 = f32[32,1,32768]{2,1,0:T(1,128)} reshape(f32[4096,8,32]{2,1,0:T(8,128)} %bitcast.85) | data formatting | bytes 8388608
  472.4 61.1 %all_to_all.33 = f32[32,1,32768]{2,1,0:T(1,128)} all-to-all(f32[32,1,32768]{2,1,0:T(1,128)} %reshape.47), channel_id=1, replica_groups=mesh['ang'=4,'pix'=32] {'pix'}, dimensions={0} | all-to-all | bytes 8388608 | tf_op jit(solution)/shard_map/all_to_all | solution.py:59
  534.1 13.7 %reduce.4 = f32[32,32768]{1,0:T(8,128)} reduce(f32[32,1,32768]{2,1,0:T(1,128)} %all_to_all.33, f32[]{:T(128)} %broadcast.81), dimensions={1}, to_apply=%all_to_all.27.reduce_sub_computation | reduce | bytes 8388612 | tf_op jit(solution)/shard_map/all_to_all | solution.py:59
  547.8 9.8 %reshape.48 = f32[4096,8,32]{2,1,0:T(8,128)} reshape(f32[32,32768]{1,0:T(8,128)} %reduce.4) | data formatting | bytes 8388608
  557.6 12.1 %copy.44 = f32[32,32,8,128]{3,2,1,0:T(8,128)} copy(f32[32,32,8,128]{0,2,3,1:T(8,128)} %bitcast.86) | data formatting | bytes 8388608 | tf_op jit(solution)/shard_map/all_to_all | solution.py:59
  (55 shorter events, 42.6 us)
Async XLA Ops:
  6.5 175.1 %copy-start = (f32[256,48]{0,1:T(8,128)S(1)}, f32[256,48]{0,1:T(8,128)}, u32[]{:S(2)}) copy-start(f32[256,48]{0,1:T(8,128)} %param.8) | copy-start | bytes 147460
  6.5 133.6 %all-reduce.3.cloned.1.call-start = ((), (), s32[]{:S(2)}) async-start(), calls=%async_computation.2 | async-start | bytes 524288 | tf_op jit(solution)/shard_map/psum | solution.py:11
  14.8 3.2 copy-start.2
  35.3 146.4 %all-reduce.5.cloned.1.call-start = ((), (), s32[]{:S(2)}) async-start(), calls=%async_computation.3 | async-start | bytes 524288 | tf_op jit(solution)/shard_map/psum | solution.py:12
  140.2 158.4 %all-gather.2.cloned.1.call-start = ((), (), s32[]{:S(2)}) async-start(), calls=%async_computation.4 | async-start | bytes 7864320 | tf_op jit(solution)/shard_map/all_gather | solution.py:45
  223.0 21.0 %copy-start.5 = (f32[256,256]{1,0:T(8,128)S(1)}, f32[256,256]{1,0:T(8,128)}, u32[]{:S(2)}) copy-start(f32[256,256]{1,0:T(8,128)} %all-reduce.5.cloned.1.call-done) | copy-start | bytes 786436
  223.0 62.2 %all-to-all-start = ((f32[32,256,128]{2,0,1:T(8,128)}), f32[32,256,128]{2,0,1:T(8,128)}, u32[]{:S(2)}, u32[]{:S(2)}) async-start(f32[32,256,128]{2,0,1:T(8,128)} %copy.33), calls=%async_computation | async-start | bytes 8388608 | tf_op jit(solution)/shard_map/all_to_all | solution.py:43
  298.5 6.0 %copy-start.4 = (f32[32,8,32,128]{3,2,1,0:T(8,128)S(1)}, f32[32,8,32,128]{3,2,1,0:T(8,128)}, u32[]{:S(2)}) copy-start(f32[32,8,32,128]{3,2,1,0:T(8,128)} %bitcast_subtract_fusion) | copy-start | bytes 12582916
  301.9 2.7 copy-start.3
  557.6 12.1 %copy-start.1 = (f32[256,48]{0,1:T(8,128)S(1)}, f32[256,48]{0,1:T(8,128)}, u32[]{:S(2)}) copy-start(f32[256,48]{0,1:T(8,128)} %param.8) | copy-start | bytes 147460
Sparse Core Ops, SparseCore 0:
  35.4 104.6 all-reduce.2
  142.6 39.0 all-reduce.4
  216.5 69.2 all-gather.1
